TPU v7x, 128 devices: a whole 4x4x4 slice. The times are simulated.
128 devices in a mesh: gx: 8 (over x, y_hi), gy: 16 (over z, y_lo, core).
Axes of the slice: x: 4, y: 4 (y_hi: 2, y_lo: 2; y = y_hi * 2 + y_lo), z: 4, core: 2. Of those that a mesh axis runs over, the one named last changes fastest.
Arguments:
- picture_embeds: bfloat16 [131072, 1152], P(('gx', 'gy')), may hold values from -6 to 6
- motion_embeds: bfloat16 [131072, 1152], P(('gx', 'gy')), may hold values from -6 to 6
- match_indices: int32 [128, 1024], P(('gx', 'gy')), may hold values from 0 to 1023, each once within a row
- sharpness_coefficient: float32 [1], replicated, may hold values from 0.04 to 0.12
- additive_shift: float32 [1], replicated, may hold values from -3 to -1
- precision_gain: float32 [1], replicated, may hold values from 65536 to 262144
Outputs:
- grad_image: bfloat16 [131072, 1152], P(('gx', 'gy'))
- grad_sensor: bfloat16 [131072, 1152], P(('gx', 'gy'))
Inputs may be any that keep to these rules, and one draw needn't show every extreme that they name: Each row of match_indices is a permutation of 0 to 1023.
All inputs are finite; a program needn't handle non-finite values.
Results may differ from a plain program's by a relative error of at most 0.0038.
Values may be sent and summed in bfloat16 or wider, within the bound.
No kernel may reach another device: no remote copies, remote signals or barrier semaphores. Data moves between devices by JAX's collectives and lax.ppermute only.
A program may use at most 128 MiB of HBM per device.

v0:
```python
import jax
import jax.numpy as jnp
from jax import lax
from jax.sharding import PartitionSpec as P


RING = ("gx", "gy")


def shifted(value, by):
    devices = lax.axis_size(RING)
    return lax.ppermute(value, RING, [(i, (i + by) % devices) for i in range(devices)])


def pairing_weights(rows, cols, sharpness_coefficient, additive_shift, objective_coefficient, match_target):
    similarity_grid = lax.dot_general(
        rows, cols, (((1,), (1,)), ((), ())), preferred_element_type=jnp.float32
    )
    logistic_derivative = jax.nn.sigmoid(sharpness_coefficient[0] * similarity_grid + additive_shift[0])
    if match_target is not None:
        logistic_derivative = logistic_derivative - match_target
    return lax.optimization_barrier((objective_coefficient * logistic_derivative).astype(jnp.bfloat16))


def apply_rows(weights, entries):
    return jnp.dot(weights, entries, preferred_element_type=jnp.float32)


def apply_cols(weights, entries):
    return lax.dot_general(
        weights, entries, (((0,), (0,)), ((), ())), preferred_element_type=jnp.float32
    )


def per_device(picture_embeds, motion_embeds, match_indices, sharpness_coefficient, additive_shift, precision_gain):
    row_count = picture_embeds.shape[0]
    entire_height = row_count * lax.axis_size(RING)
    objective_coefficient = precision_gain[0] * sharpness_coefficient[0] / entire_height
    columns = jnp.arange(row_count, dtype=jnp.int32)
    match_target = (match_indices[0][:, None] == columns[None, :]).astype(jnp.float32)

    motion_next = shifted(motion_embeds, -1)
    picture_prev = shifted(picture_embeds, 1)
    motion_prev = shifted(motion_embeds, 1)
    picture_next = shifted(picture_embeds, -1)
    half = row_count // 2
    motion_next2_parts = [shifted(motion_next[:half], -1), shifted(motion_next[half:], -1)]
    picture_prev2 = shifted(picture_prev, 1)

    def weights_of(rows, cols, target=None):
        return pairing_weights(rows, cols, sharpness_coefficient, additive_shift, objective_coefficient, target)

    local_weights = weights_of(picture_embeds, motion_embeds, match_target)
    grad_img = apply_rows(local_weights, motion_embeds)
    grad_img = grad_img + apply_rows(weights_of(picture_embeds, motion_prev), motion_prev)
    grad_img = grad_img + apply_rows(weights_of(picture_embeds, motion_next), motion_next)
    grad_img = lax.optimization_barrier(grad_img)
    grad_sen = apply_cols(local_weights, picture_embeds)
    grad_sen = grad_sen + apply_cols(weights_of(picture_prev, motion_embeds), picture_prev)
    grad_sen = grad_sen + apply_cols(weights_of(picture_next, motion_embeds), picture_next)
    grad_sen = grad_sen + apply_cols(weights_of(picture_prev2, motion_embeds), picture_prev2)
    grad_sen = grad_sen.astype(jnp.bfloat16)
    for motion_part in motion_next2_parts:
        grad_img = grad_img + apply_rows(weights_of(picture_embeds, motion_part), motion_part)
    return (grad_img.astype(jnp.bfloat16), grad_sen)


def solution(mesh):
    return jax.shard_map(
        per_device,
        mesh=mesh,
        in_specs=(P(RING, None), P(RING, None), P(RING, None), P(), P(), P()),
        out_specs=(P(RING, None), P(RING, None)),
        check_vma=False,
    )
```

profile of v0, /device:TPU:102, one launch (start us, length us, event | category | flops | bytes accessed | tf_op | source)
XLA Modules:
  0.0 179.2 jit_solution(3431471028877831202)
XLA Ops:
  0.7 2.6 %collective-permute-start.5 = (bf16[1024,1152]{1,0:T(8,128)(2,1)}, bf16[1024,1152]{1,0:T(8,128)(2,1)}, u32[]{:S(2)}, u32[]{:S(2)}) collective-permute-start(bf16[1024,1152]{1,0:T(8,128)(2,1)} %param.6), channel_id=1, source_target_pairs={{0,127},{1,0},{2,1},{3,2},{4,3},{5,4},{6,5},{7,6},{8,7},{9,8},{10,... | collective-permute-start | bytes 7077896 | tf_op jit(solution)/shard_map/ppermute | solution.py:12
  3.3 2.6 %collective-permute-start.1 = (bf16[1024,1152]{1,0:T(8,128)(2,1)}, bf16[1024,1152]{1,0:T(8,128)(2,1)S(1)}, u32[]{:S(2)}, u32[]{:S(2)}) collective-permute-start(bf16[1024,1152]{1,0:T(8,128)(2,1)} %param.7), channel_id=1, source_target_pairs={{0,127},{1,0},{2,1},{3,2},{4,3},{5,4},{6,5},{7,6},{8,7},{9,8},{10,... | collective-permute-start | bytes 7077896 | tf_op jit(solution)/shard_map/ppermute | solution.py:12
  7.9 6.3 %multiply_convert_fusion.5 = bf16[1024,1024]{1,0:T(8,128)(2,1)S(1)} fusion(bf16[1024,1152]{1,0:T(8,128)(2,1)} %param.6, bf16[1024,1152]{1,0:T(8,128)(2,1)} %param.7, s32[1024]{0:T(1024)} %bitcast.56, f32[]{:T(128)} %bitcast.47, f32[]{:T(128)} %bitcast.39, f32[]{:T(128)S(6)} %div.27), kind=kOutput, calls=%fused_computation.8 | convolution fusion | flops 2426404864 | bytes 6819852 | tf_op jit(solution)/shard_map/dot_general | solution.py:16
  14.2 3.0 %fusion.4 = f32[1024,1152]{1,0:T(8,128)S(1)} fusion(bf16[1024,1024]{1,0:T(8,128)(2,1)S(1)} %multiply_convert_fusion.5, bf16[1024,1152]{1,0:T(8,128)(2,1)S(1)} %copy-done), kind=kOutput, calls=%fused_computation.16 | convolution fusion | flops 2415919104 | bytes 9175040 | tf_op jit(solution)/shard_map/dot_general | solution.py:30
  17.3 2.9 %fusion.1 = f32[1024,1152]{1,0:T(8,128)S(1)} fusion(bf16[1024,1024]{1,0:T(8,128)(2,1)S(1)} %multiply_convert_fusion.5, bf16[1024,1152]{1,0:T(8,128)(2,1)S(1)} %copy-done.1), kind=kOutput, calls=%fused_computation.13 | convolution fusion | flops 2415919104 | bytes 9175040 | tf_op jit(solution)/shard_map/dot_general | solution.py:26
  20.2 34.5 %collective-permute-done.4 = bf16[1024,1152]{1,0:T(8,128)(2,1)} collective-permute-done((bf16[1024,1152]{1,0:T(8,128)(2,1)}, bf16[1024,1152]{1,0:T(8,128)(2,1)}, u32[]{:S(2)}, u32[]{:S(2)}) %collective-permute-start.4) | collective-permute-done | bytes 2359328 | tf_op jit(solution)/shard_map/ppermute | solution.py:12
  54.7 6.3 %multiply_convert_fusion.2 = bf16[1024,1024]{1,0:T(8,128)(2,1)} fusion(bf16[1024,1152]{1,0:T(8,128)(2,1)} %collective-permute-done.4, bf16[1024,1152]{1,0:T(8,128)(2,1)S(1)} %copy-done.1, f32[]{:T(128)} %bitcast.51, f32[]{:T(128)} %bitcast.43, f32[]{:T(128)S(6)} %div.27), kind=kOutput, calls=%fused_computation.5 | convolution fusion | flops 2423259136 | bytes 6815756 | tf_op jit(solution)/shard_map/dot_general | solution.py:16
  61.0 6.3 %multiply_convert_fusion.1 = bf16[1024,1024]{1,0:T(8,128)(2,1)} fusion(bf16[1024,1152]{1,0:T(8,128)(2,1)} %collective-permute-done.5, bf16[1024,1152]{1,0:T(8,128)(2,1)S(1)} %copy-done.1, f32[]{:T(128)} %bitcast.50, f32[]{:T(128)} %bitcast.42, f32[]{:T(128)S(6)} %div.27), kind=kOutput, calls=%fused_computation.4 | convolution fusion | flops 2423259136 | bytes 6815756 | tf_op jit(solution)/shard_map/dot_general | solution.py:16
  67.3 37.9 %collective-permute-done = bf16[1024,1152]{1,0:T(8,128)(2,1)} collective-permute-done((bf16[1024,1152]{1,0:T(8,128)(2,1)}, bf16[1024,1152]{1,0:T(8,128)(2,1)}, u32[]{:S(2)}, u32[]{:S(2)}) %collective-permute-start) | collective-permute-done | bytes 2359328 | tf_op jit(solution)/shard_map/ppermute | solution.py:12
  105.2 5.3 %multiply_convert_fusion.4 = bf16[1024,1024]{1,0:T(8,128)(2,1)S(1)} fusion(bf16[1024,1152]{1,0:T(8,128)(2,1)S(1)} %copy-done, bf16[1024,1152]{1,0:T(8,128)(2,1)} %collective-permute-done, f32[]{:T(128)} %bitcast.53, f32[]{:T(128)} %bitcast.45, f32[]{:T(128)S(6)} %div.27), kind=kOutput, calls=%fused_computation.7 | convolution fusion | flops 2423259136 | bytes 6815756 | tf_op jit(solution)/shard_map/dot_general | solution.py:16
  110.5 3.7 %multiply_convert_fusion.3 = bf16[1024,1024]{1,0:T(8,128)(2,1)S(1)} fusion(bf16[1024,1152]{1,0:T(8,128)(2,1)S(1)} %copy-done, bf16[1024,1152]{1,0:T(8,128)(2,1)S(1)} %collective-permute-done.1, f32[]{:T(128)} %bitcast.52, f32[]{:T(128)} %bitcast.44, f32[]{:T(128)S(6)} %div.27), kind=kOutput, calls=%fused_computation.6 | convolution fusion | flops 2423259136 | bytes 6815756 | tf_op jit(solution)/shard_map/dot_general | solution.py:16
  114.6 0.5 collective-permute-start.6
  115.1 4.5 %fusion.2 = f32[1024,1152]{1,0:T(8,128)S(1)} fusion(bf16[1024,1024]{1,0:T(8,128)(2,1)S(1)} %multiply_convert_fusion.4, bf16[1024,1152]{1,0:T(8,128)(2,1)} %collective-permute-done), kind=kOutput, calls=%fused_computation.14 | convolution fusion | flops 2415919104 | bytes 9175040 | tf_op jit(solution)/shard_map/dot_general | solution.py:26
  119.6 3.0 %add_add_fusion = f32[1024,1152]{1,0:T(8,128)S(1)} fusion(f32[1024,1152]{1,0:T(8,128)S(1)} %fusion.1, f32[1024,1152]{1,0:T(8,128)S(1)} %fusion.2, bf16[1024,1024]{1,0:T(8,128)(2,1)S(1)} %multiply_convert_fusion.3, bf16[1024,1152]{1,0:T(8,128)(2,1)S(1)} %collective-permute-done.1), kind=kOutput, calls=%fused_computation.2 | convolution fusion | flops 2418278400 | bytes 18612224 | tf_op jit(solution)/shard_map/dot_general | solution.py:26
  122.6 5.4 %fusion.5 = f32[1024,1152]{1,0:T(8,128)S(1)} fusion(bf16[1024,1024]{1,0:T(8,128)(2,1)} %multiply_convert_fusion.2, bf16[1024,1152]{1,0:T(8,128)(2,1)} %collective-permute-done.4), kind=kOutput, calls=%fused_computation.17 | convolution fusion | flops 2415919104 | bytes 9175040 | tf_op jit(solution)/shard_map/dot_general | solution.py:30
  128.1 4.7 %fusion.6 = f32[1024,1152]{1,0:T(8,128)S(1)} fusion(bf16[1024,1024]{1,0:T(8,128)(2,1)S(1)} %copy-done.2, bf16[1024,1152]{1,0:T(8,128)(2,1)} %collective-permute-done.5), kind=kOutput, calls=%fused_computation.18 | convolution fusion | flops 2415919104 | bytes 9175040 | tf_op jit(solution)/shard_map/dot_general | solution.py:30
  132.8 6.3 %collective-permute-done.2 = bf16[512,1152]{1,0:T(8,128)(2,1)S(1)} collective-permute-done((bf16[512,1152]{1,0:T(8,128)(2,1)S(1)}, bf16[512,1152]{1,0:T(8,128)(2,1)S(1)}, u32[]{:S(2)}, u32[]{:S(2)}) %collective-permute-start.2) | collective-permute-done | bytes 1179680 | tf_op jit(solution)/shard_map/ppermute | solution.py:12
  139.1 1.8 %multiply_convert_fusion.7 = bf16[1024,512]{1,0:T(8,128)(2,1)S(1)} fusion(bf16[1024,1152]{1,0:T(8,128)(2,1)S(1)} %copy-done, bf16[512,1152]{1,0:T(8,128)(2,1)S(1)} %collective-permute-done.2, f32[]{:T(128)} %bitcast.48, f32[]{:T(128)} %bitcast.40, f32[]{:T(128)S(6)} %div.27), kind=kOutput, calls=%fused_computation.11 | convolution fusion | flops 1211629568 | bytes 4587532 | tf_op jit(solution)/shard_map/dot_general | solution.py:16
  140.9 23.4 %collective-permute-done.3 = bf16[512,1152]{1,0:T(8,128)(2,1)S(1)} collective-permute-done((bf16[512,1152]{1,0:T(8,128)(2,1)S(1)}, bf16[512,1152]{1,0:T(8,128)(2,1)S(1)}, u32[]{:S(2)}, u32[]{:S(2)}) %collective-permute-start.3) | collective-permute-done | bytes 1179680 | tf_op jit(solution)/shard_map/ppermute | solution.py:12
  164.4 2.1 %multiply_convert_fusion.6 = bf16[1024,512]{1,0:T(8,128)(2,1)S(1)} fusion(bf16[1024,1152]{1,0:T(8,128)(2,1)S(1)} %copy-done, bf16[512,1152]{1,0:T(8,128)(2,1)S(1)} %collective-permute-done.3, f32[]{:T(128)} %bitcast.54, f32[]{:T(128)} %bitcast.46, f32[]{:T(128)S(6)} %div.27), kind=kOutput, calls=%fused_computation.10 | convolution fusion | flops 1211629568 | bytes 4587532 | tf_op jit(solution)/shard_map/dot_general | solution.py:16
  166.5 1.5 fusion.3
  168.0 2.9 %add_convert_fusion.1 = bf16[1024,1152]{1,0:T(8,128)(2,1)} fusion(f32[1024,1152]{1,0:T(8,128)S(1)} %add_add_fusion, f32[1024,1152]{1,0:T(8,128)S(1)} %fusion.3, bf16[1024,512]{1,0:T(8,128)(2,1)S(1)} %multiply_convert_fusion.6, bf16[512,1152]{1,0:T(8,128)(2,1)S(1)} %collective-permute-done.3), kind=kOutput, calls=%fused_computation.1 | convolution fusion | flops 1211498496 | bytes 14024704 | tf_op jit(solution)/shard_map/dot_general | solution.py:26
  171.0 3.7 %multiply_convert_fusion = bf16[1024,1024]{1,0:T(8,128)(2,1)S(1)} fusion(bf16[1024,1152]{1,0:T(8,128)(2,1)S(1)} %collective-permute-done.6, bf16[1024,1152]{1,0:T(8,128)(2,1)S(1)} %copy-done.1, f32[]{:T(128)} %bitcast.49, f32[]{:T(128)} %bitcast.41, f32[]{:T(128)S(6)} %div.27), kind=kOutput, calls=%fused_computation.3 | convolution fusion | flops 2423259136 | bytes 6815756 | tf_op jit(solution)/shard_map/dot_general | solution.py:16
  174.7 4.5 %add_convert_fusion = bf16[1024,1152]{1,0:T(8,128)(2,1)} fusion(f32[1024,1152]{1,0:T(8,128)S(1)} %fusion.6, f32[1024,1152]{1,0:T(8,128)S(1)} %fusion.4, f32[1024,1152]{1,0:T(8,128)S(1)} %fusion.5, bf16[1024,1024]{1,0:T(8,128)(2,1)S(1)} %multiply_convert_fusion, bf16[1024,1152]{1,0:T(8,128)(2,1)S(1)} %collective-permute-done.6), kind=kOutput, calls=%fused_computation | convolution fusion | flops 2420637696 | bytes 20971520 | tf_op jit(solution)/shard_map/dot_general | solution.py:30
  (14 shorter events, 0.4 us)
Async XLA Ops:
  0.6 54.0 %collective-permute-start.4 = (bf16[1024,1152]{1,0:T(8,128)(2,1)}, bf16[1024,1152]{1,0:T(8,128)(2,1)}, u32[]{:S(2)}, u32[]{:S(2)}) collective-permute-start(bf16[1024,1152]{1,0:T(8,128)(2,1)} %param.6), channel_id=1, source_target_pairs={{0,1},{1,2},{2,3},{3,4},{4,5},{5,6},{6,7},{7,8},{8,9},{9,10},{10,1... | collective-permute-start | bytes 7077896 | tf_op jit(solution)/shard_map/ppermute | solution.py:12
  0.7 60.3 %collective-permute-start.5 = (bf16[1024,1152]{1,0:T(8,128)(2,1)}, bf16[1024,1152]{1,0:T(8,128)(2,1)}, u32[]{:S(2)}, u32[]{:S(2)}) collective-permute-start(bf16[1024,1152]{1,0:T(8,128)(2,1)} %param.6), channel_id=1, source_target_pairs={{0,127},{1,0},{2,1},{3,2},{4,3},{5,4},{6,5},{7,6},{8,7},{9,8},{10,... | collective-permute-start | bytes 7077896 | tf_op jit(solution)/shard_map/ppermute | solution.py:12
  3.3 101.9 %collective-permute-start = (bf16[1024,1152]{1,0:T(8,128)(2,1)}, bf16[1024,1152]{1,0:T(8,128)(2,1)}, u32[]{:S(2)}, u32[]{:S(2)}) collective-permute-start(bf16[1024,1152]{1,0:T(8,128)(2,1)} %param.7), channel_id=1, source_target_pairs={{0,1},{1,2},{2,3},{3,4},{4,5},{5,6},{6,7},{7,8},{8,9},{9,10},{10,1... | collective-permute-start | bytes 7077896 | tf_op jit(solution)/shard_map/ppermute | solution.py:12
  3.3 107.2 %collective-permute-start.1 = (bf16[1024,1152]{1,0:T(8,128)(2,1)}, bf16[1024,1152]{1,0:T(8,128)(2,1)S(1)}, u32[]{:S(2)}, u32[]{:S(2)}) collective-permute-start(bf16[1024,1152]{1,0:T(8,128)(2,1)} %param.7), channel_id=1, source_target_pairs={{0,127},{1,0},{2,1},{3,2},{4,3},{5,4},{6,5},{7,6},{8,7},{9,8},{10,... | collective-permute-start | bytes 7077896 | tf_op jit(solution)/shard_map/ppermute | solution.py:12
  7.9 6.3 %copy-start = (bf16[1024,1152]{1,0:T(8,128)(2,1)S(1)}, bf16[1024,1152]{1,0:T(8,128)(2,1)}, u32[]{:S(2)}) copy-start(bf16[1024,1152]{1,0:T(8,128)(2,1)} %param.6) | copy-start | bytes 7077892
  14.2 3.1 %copy-start.1 = (bf16[1024,1152]{1,0:T(8,128)(2,1)S(1)}, bf16[1024,1152]{1,0:T(8,128)(2,1)}, u32[]{:S(2)}) copy-start(bf16[1024,1152]{1,0:T(8,128)(2,1)} %param.7) | copy-start | bytes 7077892
  114.4 24.7 %collective-permute-start.2 = (bf16[512,1152]{1,0:T(8,128)(2,1)S(1)}, bf16[512,1152]{1,0:T(8,128)(2,1)S(1)}, u32[]{:S(2)}, u32[]{:S(2)}) collective-permute-start(bf16[512,1152]{1,0:T(8,128)(2,1)S(1)} %get-tuple-element.2), channel_id=1, source_target_pairs={{0,127},{1,0},{2,1},{3,2},{4,3},{5,4},{6,5},{7,6},{8,7},{9,8},{10,... | collective-permute-start | bytes 3538952 | tf_op jit(solution)/shard_map/ppermute | solution.py:12
  114.5 49.9 %collective-permute-start.3 = (bf16[512,1152]{1,0:T(8,128)(2,1)S(1)}, bf16[512,1152]{1,0:T(8,128)(2,1)S(1)}, u32[]{:S(2)}, u32[]{:S(2)}) collective-permute-start(bf16[512,1152]{1,0:T(8,128)(2,1)S(1)} %get-tuple-element.3), channel_id=1, source_target_pairs={{0,127},{1,0},{2,1},{3,2},{4,3},{5,4},{6,5},{7,6},{8,7},{9,8},{10,... | collective-permute-start | bytes 3538952 | tf_op jit(solution)/shard_map/ppermute | solution.py:12
  114.6 56.4 %collective-permute-start.6 = (bf16[1024,1152]{1,0:T(8,128)(2,1)}, bf16[1024,1152]{1,0:T(8,128)(2,1)S(1)}, u32[]{:S(2)}, u32[]{:S(2)}) collective-permute-start(bf16[1024,1152]{1,0:T(8,128)(2,1)} %collective-permute-done.4), channel_id=1, source_target_pairs={{0,1},{1,2},{2,3},{3,4},{4,5},{5,6},{6,7},{7,8},{8,9},{9,10},{10,1... | collective-permute-start | bytes 7077896 | tf_op jit(solution)/shard_map/ppermute | solution.py:12
  122.6 5.5 %copy-start.2 = (bf16[1024,1024]{1,0:T(8,128)(2,1)S(1)}, bf16[1024,1024]{1,0:T(8,128)(2,1)}, u32[]{:S(2)}) copy-start(bf16[1024,1024]{1,0:T(8,128)(2,1)} %multiply_convert_fusion.1) | copy-start | bytes 6291460
where the time goes:
time: 183 us; the launch traced here: 179 us
  waiting for transfers between devices  102 us (56%)
  matrix products  68.1 us (37%)
  starting transfers between devices  6 us (3%)
  between operations  2.75 us (2%)
    ppermute x7, waiting for transfers between devices, shifted(): lax.ppermute(value, RING, [(i, (i + by) % devices) for i in range(devices)])  102 us
    dot_general x8, matrix products, pairing_weights(): lax.dot_general(rows, cols, (((1,), (1,)), ((), ())), preferred_element_t...  35.6 us
    dot_general x4, matrix products, apply_cols(): lax.dot_general(weights, entries, (((0,), (0,)), ((), ())), preferred_ele...  17.7 us
    dot_general x5, matrix products, apply_rows(): return jnp.dot(weights, entries, preferred_element_type=jnp.float32)  14.8 us
    ppermute x7, starting transfers between devices, shifted(): lax.ppermute(value, RING, [(i, (i + by) % devices) for i in range(devices)])  6 us
  transfers between devices with their start and end apart: 7, of which 4 were waited for; matrix products, arithmetic and copies ran while one was open for 31% of the time, Pallas kernels for 0%

commit v1 on v0

--- a/solution.py
+++ b/solution.py
@@ -39,12 +39,12 @@
     columns = jnp.arange(row_count, dtype=jnp.int32)
     match_target = (match_indices[0][:, None] == columns[None, :]).astype(jnp.float32)
 
-    motion_next = shifted(motion_embeds, -1)
-    picture_prev = shifted(picture_embeds, 1)
-    motion_prev = shifted(motion_embeds, 1)
-    picture_next = shifted(picture_embeds, -1)
-    half = row_count // 2
-    motion_next2_parts = [shifted(motion_next[:half], -1), shifted(motion_next[half:], -1)]
+    stacked = jnp.concatenate([motion_embeds, picture_embeds], axis=0)
+    from_prev = shifted(stacked, 1)
+    from_next = shifted(stacked, -1)
+    motion_prev, picture_prev = from_prev[:row_count], from_prev[row_count:]
+    motion_next, picture_next = from_next[:row_count], from_next[row_count:]
+    motion_next2 = shifted(motion_next, -1)
     picture_prev2 = shifted(picture_prev, 1)
 
     def weights_of(rows, cols, target=None):
@@ -60,8 +60,7 @@
     grad_sen = grad_sen + apply_cols(weights_of(picture_next, motion_embeds), picture_next)
     grad_sen = grad_sen + apply_cols(weights_of(picture_prev2, motion_embeds), picture_prev2)
     grad_sen = grad_sen.astype(jnp.bfloat16)
-    for motion_part in motion_next2_parts:
-        grad_img = grad_img + apply_rows(weights_of(picture_embeds, motion_part), motion_part)
+    grad_img = grad_img + apply_rows(weights_of(picture_embeds, motion_next2), motion_next2)
     return (grad_img.astype(jnp.bfloat16), grad_sen)
 
 

time: 183 us -> 190 us (1.038)
  local copies, waits for them, and re-layouts: 0.2 us -> 8.77 us
  waiting for transfers between devices: 102 us -> 94.4 us
  matrix products: 68.1 us -> 74.8 us
  starting transfers between devices: 6 us -> 3.46 us
    ppermute x7 -> x4, waiting for transfers between devices: 102 us -> 94.4 us  [shifted(): lax.ppermute(value, RING, [(i, (i + by) % devices) for i in range(devices)])]
    slice x1 -> x2, local copies, waits for them, and re-layouts: 0.18 us -> 3.69 us  [the longest x1 1.85 us: per_device(): motion_prev, picture_prev = (from_prev[:row_count], from_prev[row_count:])]
    unnamed x6 -> x7, local copies, waits for them, and re-layouts: 0.02 us -> 3.39 us
    dot_general x4, matrix products: 17.7 us -> 20.9 us  [apply_cols(): lax.dot_general(weights, entries, (((0,), (0,)), ((), ())), preferred_ele...]
    dot_general x5 -> x4, matrix products: 14.8 us -> 18 us  [apply_rows(): return jnp.dot(weights, entries, preferred_element_type=jnp.float32)]
    ppermute x7 -> x4, starting transfers between devices: 6 us -> 3.46 us  [shifted(): lax.ppermute(value, RING, [(i, (i + by) % devices) for i in range(devices)])]
    dot_general x8 -> x7, matrix products: 35.6 us -> 35.9 us  [pairing_weights(): lax.dot_general(rows, cols, (((1,), (1,)), ((), ())), preferred_element_t...]
  transfers between devices with their start and end apart: 7 -> 4, of which waited for: 4 -> 2; matrix products, arithmetic and copies ran while one was open for 31% -> 34% of each run, Pallas kernels for 0% -> 0%
where the time goes in v1:
time: 190 us; the launch traced here: 186 us
  waiting for transfers between devices  94.4 us (50%)
  matrix products  74.8 us (39%)
  local copies, waits for them, and re-layouts  8.77 us (5%)
  starting transfers between devices  3.46 us (2%)
  between operations  2.74 us (1%)
    ppermute x4, waiting for transfers between devices, shifted(): lax.ppermute(value, RING, [(i, (i + by) % devices) for i in range(devices)])  94.4 us
    dot_general x7, matrix products, pairing_weights(): lax.dot_general(rows, cols, (((1,), (1,)), ((), ())), preferred_element_t...  35.9 us
    dot_general x4, matrix products, apply_cols(): lax.dot_general(weights, entries, (((0,), (0,)), ((), ())), preferred_ele...  20.9 us
    dot_general x4, matrix products, apply_rows(): return jnp.dot(weights, entries, preferred_element_type=jnp.float32)  18 us
  transfers between devices with their start and end apart: 4, of which 2 were waited for; matrix products, arithmetic and copies ran while one was open for 34% of the time, Pallas kernels for 0%

profile of v1, /device:TPU:102, one launch (start us, length us, event | category | flops | bytes accessed | tf_op | source)
XLA Modules:
  0.0 186.1 jit_solution(14187846675075881084)
XLA Ops:
  0.6 3.4 %constant_dynamic-update-slice_fusion.1 = bf16[2048,1152]{1,0:T(8,128)(2,1)} fusion(bf16[1024,1152]{1,0:T(8,128)(2,1)} %param.7), kind=kLoop, calls=%fused_computation.21 | loop fusion | bytes 4718592
  4.0 1.7 constant_dynamic-update-slice_fusion
  5.7 2.6 %collective-permute-start.1 = (bf16[2048,1152]{1,0:T(8,128)(2,1)}, bf16[2048,1152]{1,0:T(8,128)(2,1)}, u32[]{:S(2)}, u32[]{:S(2)}) collective-permute-start(bf16[2048,1152]{1,0:T(8,128)(2,1)} %constant_dynamic-update-slice_fusion), channel_id=1, source_target_pairs={{0,127},{1,0},{2,1},{3,2},{4,3},{5,4},{6,5},{7,6},{8,7},{9,8},{10,... | collective-permute-start | bytes 14155784 | tf_op jit(solution)/shard_map/ppermute | solution.py:12
  10.3 5.8 %multiply_convert_fusion.6 = bf16[1024,1024]{1,0:T(8,128)(2,1)S(1)} fusion(bf16[1024,1152]{1,0:T(8,128)(2,1)S(1)} %copy-done, bf16[1024,1152]{1,0:T(8,128)(2,1)} %param.7, s32[1024]{0:T(1024)S(1)} %bitcast.48, f32[]{:T(128)} %bitcast.40, f32[]{:T(128)} %bitcast.33, f32[]{:T(128)S(6)} %div.24), kind=kOutput, calls=%fused_computation.9 | convolution fusion | flops 2426404864 | bytes 6819852 | tf_op jit(solution)/shard_map/dot_general | solution.py:16
  16.2 2.9 %fusion.16 = f32[1024,1152]{1,0:T(8,128)S(1)} fusion(bf16[1024,1024]{1,0:T(8,128)(2,1)S(1)} %multiply_convert_fusion.6, bf16[1024,1152]{1,0:T(8,128)(2,1)S(1)} %copy-done.1), kind=kOutput, calls=%fused_computation.27 | convolution fusion | flops 2415919104 | bytes 9175040 | tf_op jit(solution)/shard_map/dot_general | solution.py:26
  19.0 3.0 %fusion.18 = f32[1024,1152]{1,0:T(8,128)S(1)} fusion(bf16[1024,1024]{1,0:T(8,128)(2,1)S(1)} %multiply_convert_fusion.6, bf16[1024,1152]{1,0:T(8,128)(2,1)S(1)} %copy-done), kind=kOutput, calls=%fused_computation.29 | convolution fusion | flops 2415919104 | bytes 9175040 | tf_op jit(solution)/shard_map/dot_general | solution.py:30
  22.1 88.2 %collective-permute-done = bf16[2048,1152]{1,0:T(8,128)(2,1)} collective-permute-done((bf16[2048,1152]{1,0:T(8,128)(2,1)}, bf16[2048,1152]{1,0:T(8,128)(2,1)}, u32[]{:S(2)}, u32[]{:S(2)}) %collective-permute-start) | collective-permute-done | bytes 4718624 | tf_op jit(solution)/shard_map/ppermute | solution.py:12
  110.2 5.4 %fusion.6 = bf16[1024,1024]{0,1:T(8,128)(2,1)S(1)} fusion(f32[]{:T(128)} %bitcast.46, bf16[1024,1152]{1,0:T(8,128)(2,1)S(1)} %copy-done, bf16[2048,1152]{1,0:T(8,128)(2,1)} %collective-permute-done, f32[]{:T(128)} %bitcast.39, f32[]{:T(128)S(6)} %div.24), kind=kOutput, calls=%fused_computation.17 | convolution fusion | flops 2423259136 | bytes 6816772 | tf_op jit(solution)/shard_map/dot_general | solution.py:16
  115.6 1.8 slice.17
  117.5 1.8 slice.18
  119.4 0.7 collective-permute-start.3
  120.1 5.4 %fusion.9 = bf16[1024,1024]{0,1:T(8,128)(2,1)S(1)} fusion(f32[]{:T(128)} %bitcast.45, bf16[1024,1152]{1,0:T(8,128)(2,1)S(1)} %copy-done, f32[]{:T(128)} %bitcast.38, f32[]{:T(128)S(6)} %div.24, bf16[2048,1152]{1,0:T(8,128)(2,1)} %collective-permute-done.1), kind=kOutput, calls=%fused_computation.18 | convolution fusion | flops 2423259136 | bytes 6816772 | tf_op jit(solution)/shard_map/dot_general | solution.py:16
  125.5 6.4 %multiply_convert_fusion.4 = bf16[1024,1024]{1,0:T(8,128)(2,1)} fusion(bf16[1024,1152]{1,0:T(8,128)(2,1)S(1)} %copy-done.1, f32[]{:T(128)} %bitcast.42, f32[]{:T(128)} %bitcast.35, f32[]{:T(128)S(6)} %div.24, bf16[2048,1152]{1,0:T(8,128)(2,1)} %collective-permute-done.1), kind=kOutput, calls=%fused_computation.7 | convolution fusion | flops 2423259136 | bytes 6816772 | tf_op jit(solution)/shard_map/dot_general | solution.py:16
  131.9 5.4 %multiply_convert_fusion.5 = bf16[1024,1024]{1,0:T(8,128)(2,1)S(1)} fusion(bf16[1024,1152]{1,0:T(8,128)(2,1)S(1)} %copy-done.1, f32[]{:T(128)} %bitcast.43, f32[]{:T(128)} %bitcast.36, f32[]{:T(128)S(6)} %div.24, bf16[2048,1152]{1,0:T(8,128)(2,1)} %collective-permute-done), kind=kOutput, calls=%fused_computation.8 | convolution fusion | flops 2423259136 | bytes 6816772 | tf_op jit(solution)/shard_map/dot_general | solution.py:16
  137.3 6.4 %fusion.3 = f32[1024,1152]{1,0:T(8,128)} fusion(bf16[1024,1024]{0,1:T(8,128)(2,1)S(1)} %fusion.6, bf16[2048,1152]{1,0:T(8,128)(2,1)} %collective-permute-done), kind=kOutput, calls=%fused_computation.14 | convolution fusion | flops 2415919104 | bytes 9175040 | tf_op jit(solution)/shard_map/dot_general | solution.py:26
  143.6 5.7 %add_add_fusion = f32[1024,1152]{1,0:T(8,128)S(1)} fusion(f32[1024,1152]{1,0:T(8,128)S(1)} %fusion.16, f32[1024,1152]{1,0:T(8,128)} %fusion.3, bf16[1024,1024]{0,1:T(8,128)(2,1)S(1)} %fusion.9, bf16[2048,1152]{1,0:T(8,128)(2,1)} %collective-permute-done.1), kind=kOutput, calls=%fused_computation.2 | convolution fusion | flops 2418278400 | bytes 18612224 | tf_op jit(solution)/shard_map/dot_general | solution.py:26
  149.4 5.3 %fusion = f32[1024,1152]{1,0:T(8,128)S(1)} fusion(bf16[1024,1024]{1,0:T(8,128)(2,1)} %multiply_convert_fusion.4, bf16[2048,1152]{1,0:T(8,128)(2,1)} %collective-permute-done.1), kind=kOutput, calls=%fused_computation.11 | convolution fusion | flops 2415919104 | bytes 9175040 | tf_op jit(solution)/shard_map/dot_general | solution.py:30
  154.7 6.3 %fusion.11 = f32[1024,1152]{1,0:T(8,128)} fusion(bf16[1024,1024]{1,0:T(8,128)(2,1)S(1)} %multiply_convert_fusion.5, bf16[2048,1152]{1,0:T(8,128)(2,1)} %collective-permute-done), kind=kOutput, calls=%fused_computation.22 | convolution fusion | flops 2415919104 | bytes 9175040 | tf_op jit(solution)/shard_map/dot_general | solution.py:30
  161.0 6.3 %collective-permute-done.2 = bf16[1024,1152]{1,0:T(8,128)(2,1)S(1)} collective-permute-done((bf16[1024,1152]{1,0:T(8,128)(2,1)S(1)}, bf16[1024,1152]{1,0:T(8,128)(2,1)S(1)}, u32[]{:S(2)}, u32[]{:S(2)}) %collective-permute-start.2) | collective-permute-done | bytes 2359328 | tf_op jit(solution)/shard_map/ppermute | solution.py:12
  167.3 3.7 %fusion.10 = bf16[1024,1024]{0,1:T(8,128)(2,1)S(1)} fusion(f32[]{:T(128)} %bitcast.44, bf16[1024,1152]{1,0:T(8,128)(2,1)S(1)} %collective-permute-done.2, bf16[1024,1152]{1,0:T(8,128)(2,1)S(1)} %copy-done, f32[]{:T(128)} %bitcast.37, f32[]{:T(128)S(6)} %div.24), kind=kOutput, calls=%fused_computation.19 | convolution fusion | flops 2423259136 | bytes 6815756 | tf_op jit(solution)/shard_map/dot_general | solution.py:16
  171.0 3.9 %multiply_convert_fusion.3 = bf16[1024,1024]{1,0:T(8,128)(2,1)S(1)} fusion(bf16[1024,1152]{1,0:T(8,128)(2,1)S(1)} %collective-permute-done.3, bf16[1024,1152]{1,0:T(8,128)(2,1)S(1)} %copy-done.1, f32[]{:T(128)} %bitcast.41, f32[]{:T(128)} %bitcast.34, f32[]{:T(128)S(6)} %div.24), kind=kOutput, calls=%fused_computation.6 | convolution fusion | flops 2423259136 | bytes 6815756 | tf_op jit(solution)/shard_map/dot_general | solution.py:16
  174.9 3.0 %fusion.17 = f32[1024,1152]{1,0:T(8,128)S(1)} fusion(bf16[1024,1024]{0,1:T(8,128)(2,1)S(1)} %fusion.10, bf16[1024,1152]{1,0:T(8,128)(2,1)S(1)} %collective-permute-done.2), kind=kOutput, calls=%fused_computation.28 | convolution fusion | flops 2415919104 | bytes 9175040 | tf_op jit(solution)/shard_map/dot_general | solution.py:26
  178.0 1.8 add_convert_fusion.1
  179.8 6.3 %add_convert_fusion = bf16[1024,1152]{1,0:T(8,128)(2,1)} fusion(f32[1024,1152]{1,0:T(8,128)S(1)} %fusion, f32[1024,1152]{1,0:T(8,128)S(1)} %fusion.18, f32[1024,1152]{1,0:T(8,128)} %fusion.11, bf16[1024,1024]{1,0:T(8,128)(2,1)S(1)} %multiply_convert_fusion.3, bf16[1024,1152]{1,0:T(8,128)(2,1)S(1)} %collective-permute-done.3), kind=kOutput, calls=%fused_computation | convolution fusion | flops 2420637696 | bytes 20971520 | tf_op jit(solution)/shard_map/dot_general | solution.py:30
  (10 shorter events, 0.1 us)
Async XLA Ops:
  0.6 3.4 %copy-start = (bf16[1024,1152]{1,0:T(8,128)(2,1)S(1)}, bf16[1024,1152]{1,0:T(8,128)(2,1)}, u32[]{:S(2)}) copy-start(bf16[1024,1152]{1,0:T(8,128)(2,1)} %param.6) | copy-start | bytes 7077892
  0.6 9.7 %copy-start.2 = (s32[1,1024]{1,0:T(1,128)S(1)}, s32[1,1024]{1,0:T(1,128)}, u32[]{:S(2)}) copy-start(s32[1,1024]{1,0:T(1,128)} %param.8) | copy-start | bytes 12292
  5.7 104.5 %collective-permute-start = (bf16[2048,1152]{1,0:T(8,128)(2,1)}, bf16[2048,1152]{1,0:T(8,128)(2,1)}, u32[]{:S(2)}, u32[]{:S(2)}) collective-permute-start(bf16[2048,1152]{1,0:T(8,128)(2,1)} %constant_dynamic-update-slice_fusion), channel_id=1, source_target_pairs={{0,1},{1,2},{2,3},{3,4},{4,5},{5,6},{6,7},{7,8},{8,9},{9,10},{10,1... | collective-permute-start | bytes 14155784 | tf_op jit(solution)/shard_map/ppermute | solution.py:12
  5.7 109.9 %collective-permute-start.1 = (bf16[2048,1152]{1,0:T(8,128)(2,1)}, bf16[2048,1152]{1,0:T(8,128)(2,1)}, u32[]{:S(2)}, u32[]{:S(2)}) collective-permute-start(bf16[2048,1152]{1,0:T(8,128)(2,1)} %constant_dynamic-update-slice_fusion), channel_id=1, source_target_pairs={{0,127},{1,0},{2,1},{3,2},{4,3},{5,4},{6,5},{7,6},{8,7},{9,8},{10,... | collective-permute-start | bytes 14155784 | tf_op jit(solution)/shard_map/ppermute | solution.py:12
  10.3 5.8 %copy-start.1 = (bf16[1024,1152]{1,0:T(8,128)(2,1)S(1)}, bf16[1024,1152]{1,0:T(8,128)(2,1)}, u32[]{:S(2)}) copy-start(bf16[1024,1152]{1,0:T(8,128)(2,1)} %param.7) | copy-start | bytes 7077892
  117.5 49.8 %collective-permute-start.2 = (bf16[1024,1152]{1,0:T(8,128)(2,1)S(1)}, bf16[1024,1152]{1,0:T(8,128)(2,1)S(1)}, u32[]{:S(2)}, u32[]{:S(2)}) collective-permute-start(bf16[1024,1152]{1,0:T(8,128)(2,1)S(1)} %slice.17), channel_id=1, source_target_pairs={{0,127},{1,0},{2,1},{3,2},{4,3},{5,4},{6,5},{7,6},{8,7},{9,8},{10,... | collective-permute-start | bytes 7077896 | tf_op jit(solution)/shard_map/ppermute | solution.py:12
  119.4 51.6 %collective-permute-start.3 = (bf16[1024,1152]{1,0:T(8,128)(2,1)S(1)}, bf16[1024,1152]{1,0:T(8,128)(2,1)S(1)}, u32[]{:S(2)}, u32[]{:S(2)}) collective-permute-start(bf16[1024,1152]{1,0:T(8,128)(2,1)S(1)} %slice.18), channel_id=1, source_target_pairs={{0,1},{1,2},{2,3},{3,4},{4,5},{5,6},{6,7},{7,8},{8,9},{9,10},{10,1... | collective-permute-start | bytes 7077896 | tf_op jit(solution)/shard_map/ppermute | solution.py:12
